TPU v7x, 32 devices: a whole 2x2x4 slice. The times are simulated.
32 devices in a mesh: layer: 4 (over y, x), tok: 8 (over z, core).
Axes of the slice: x: 2, y: 2, z: 4, core: 2. Of those that a mesh axis runs over, the one named last changes fastest.
Arguments:
- residual: bfloat16 [4, 1024, 3584], P('layer', 'tok'), may hold values from -6 to 6
- targets: bfloat16 [4, 1024, 3584], P('layer', 'tok'), may hold values from -6 to 6
- block_ids: int32 [4, 1024, 2], P(None, 'tok'), may hold values from 0 to 127, all different within a row; in each aligned block of 128 rows (0 to 127, 128 to 255, ..., all dimensions but the last counted through in order) at most 4 rows name the same one
- encoder_weight: bfloat16 [4, 3584, 16384], P('layer', None, 'tok'), may hold values from -0.09375 to 0.09375
- encoder_bias: float32 [4, 16384], P('layer', 'tok'), may hold values from -3 to 3
- decoder_weight: bfloat16 [4, 4, 16384, 3584], P('layer', None, 'tok'), may hold values from -0.25 to 0.25
- decoder_bias: float32 [4, 3584], P('layer'), may hold values from -3 to 3
Outputs:
- reconstruction: bfloat16 [4, 1024, 3584], P('layer', 'tok')
- error: float32 [4, 1024], P('layer', 'tok')
Inputs may be any that keep to these rules, and one draw needn't show every extreme that they name: `block_ids`: A token's 2 blocks in a layer are distinct. In each layer, the 128 rows of one device (aligned blocks of tokens) name no block more than 4 times, and some block exactly 4 times.
All inputs are finite; a program needn't handle non-finite values.
Results may differ from a plain program's by a relative error of at most 0.0053.
Values may be sent and summed in bfloat16 or wider, within the bound.
No kernel may reach another device: no remote copies, remote signals or barrier semaphores. Data moves between devices by JAX's collectives and lax.ppermute only.
A program may use at most 192 MiB of HBM per device.

v0:
```python
import jax
import jax.numpy as jnp
from jax import lax
from jax.sharding import PartitionSpec as P

BLOCK = 128


def slot_positions(ids, blocks, capacity):
    flat_ids = ids.reshape(-1)
    onehot = (flat_ids[:, None] == jnp.arange(blocks, dtype=jnp.int32)[None, :]).astype(jnp.int32)
    before = jnp.cumsum(onehot, axis=0) - onehot
    rank_in = jnp.sum(before * onehot, axis=1)
    return flat_ids * capacity + rank_in


def body(residual, targets, block_ids, encoder_weight, encoder_bias, decoder_weight, decoder_bias):
    layer_index = lax.axis_index("layer")
    layers = lax.axis_size("layer")
    tok_count = lax.axis_size("tok")
    tok_rows = residual.shape[1]
    width = residual.shape[2]
    topk = block_ids.shape[2]
    per_owner = encoder_weight.shape[2] // BLOCK
    blocks = per_owner * tok_count
    capacity = max(2, 2 * tok_rows * topk // blocks)
    slot_count = blocks * capacity
    positions = jax.vmap(lambda ids: slot_positions(ids, blocks, capacity))(block_ids)
    own_positions = lax.dynamic_index_in_dim(positions, layer_index, 0, keepdims=False)
    source_row = (
        jnp.full((slot_count,), tok_rows, jnp.int32)
        .at[own_positions]
        .set(jnp.arange(tok_rows * topk, dtype=jnp.int32) // topk)
    )
    padded = jnp.concatenate([residual[0], jnp.zeros((1, width), residual.dtype)], axis=0)
    outgoing = padded[source_row].reshape(tok_count, per_owner * capacity, width)
    arrived = lax.all_to_all(outgoing, "tok", split_axis=0, concat_axis=0, tiled=True)
    arrived = arrived.reshape(tok_count, per_owner, capacity, width)
    enc_blocks = encoder_weight[0].reshape(width, per_owner, BLOCK)
    pre = jnp.einsum("sbcd,dbe->sbce", arrived, enc_blocks, preferred_element_type=jnp.float32)
    pre = pre + encoder_bias[0].reshape(per_owner, BLOCK)[None, :, None, :]
    codes = (
        jnp.maximum(pre, 0.0)
        .astype(jnp.bfloat16)
        .reshape(1, tok_count, per_owner * capacity, BLOCK)
    )
    all_codes = lax.all_gather(codes, "layer", axis=0, tiled=True)
    sources = jnp.arange(layers, dtype=jnp.int32)
    valid = sources <= layer_index
    weights = decoder_weight[0]
    keep_slot = valid.astype(jnp.float32)
    slot_sets = sources.shape[0]
    chosen_codes = (
        jnp.take(all_codes, sources, axis=0) * valid.astype(jnp.bfloat16)[:, None, None, None]
    )
    terms = (
        jnp.einsum(
            "snbce,sbed->snbcd",
            chosen_codes.reshape(slot_sets, tok_count, per_owner, capacity, BLOCK),
            weights.reshape(slot_sets, per_owner, BLOCK, width),
            preferred_element_type=jnp.float32,
        )
        .astype(jnp.bfloat16)
        .reshape(slot_sets, tok_count, per_owner * capacity, width)
    )
    returned = lax.all_to_all(terms, "tok", split_axis=1, concat_axis=1, tiled=True).reshape(
        slot_sets, slot_count, width
    )
    source_positions = jnp.take(positions, sources, axis=0)
    picked = jax.vmap(lambda rows, where_at: rows[where_at])(returned, source_positions)
    parts = jnp.sum(picked.astype(jnp.float32).reshape(slot_sets, tok_rows, topk, width), axis=2)
    own_sum = jnp.sum(parts * keep_slot[:, None, None], axis=0)
    recon32 = decoder_bias[0][None, :] + own_sum
    difference = recon32 - targets[0].astype(jnp.float32)
    error = jnp.mean(difference * difference, axis=1)
    return (recon32.astype(jnp.bfloat16)[None], error[None])


def solution(mesh):
    in_specs = (
        P("layer", "tok", None),
        P("layer", "tok", None),
        P(None, "tok", None),
        P("layer", None, "tok"),
        P("layer", "tok"),
        P("layer", None, "tok", None),
        P("layer", None),
    )
    out_specs = (P("layer", "tok", None), P("layer", "tok"))
    return jax.shard_map(body, mesh=mesh, in_specs=in_specs, out_specs=out_specs, check_vma=False)
```

profile of v0, /device:TPU:0, one launch (start us, length us, event | category | flops | bytes accessed | tf_op | source)
XLA Modules:
  0.0 584.5 jit_solution(2805510803366540468)
XLA Ops:
  0.6 0.8 copy.34
  1.5 1.0 copy.38
  2.5 0.9 fusion.14
  3.4 0.2 broadcast_add_fusion
  3.7 0.1 copy.35
  3.8 0.4 fusion.16
  4.2 1.4 scatter_custom_fusion
  5.6 1.2 concatenate.3
  6.9 4.2 gather_fusion
  11.1 6.3 %all-to-all-start = ((bf16[8,64,3584]{2,1,0:T(8,128)(2,1)}), bf16[8,64,3584]{2,1,0:T(8,128)(2,1)}, u32[]{:S(2)}, u32[]{:S(2)}) async-start(bf16[8,64,3584]{2,1,0:T(8,128)(2,1)} %bitcast.60), calls=%async_computation | async-start | bytes 7340032 | tf_op jit(solution)/shard_map/all_to_all | solution.py:37
  17.4 14.5 %copy.50 = bf16[448,8,16,128]{3,2,1,0:T(8,128)(2,1)} copy(bf16[448,8,16,128]{3,1,2,0:T(8,128)(2,1)} %bitcast.61) | data formatting | bytes 29360128
  31.9 0.0 copy-start.2
  31.9 68.3 %all-to-all-done = bf16[8,64,3584]{2,1,0:T(8,128)(2,1)} async-done(((bf16[8,64,3584]{2,1,0:T(8,128)(2,1)}), bf16[8,64,3584]{2,1,0:T(8,128)(2,1)}, u32[]{:S(2)}, u32[]{:S(2)}) %all-to-all-start) | async-done | bytes 3670048 | tf_op jit(solution)/shard_map/all_to_all | solution.py:37
  100.3 4.1 copy.40
  104.3 0.0 copy-done.2
  104.3 13.2 %fusion.11 = bf16[16,8,4,128]{3,1,2,0:T(8,128)(2,1)S(1)} fusion(bf16[8,16,4,3584]{3,0,2,1:T(8,128)(2,1)S(1)} %bitcast.63, bf16[3584,16,128,1]{2,1,0,3:T(8,128)(2,1)} %bitcast.62, f32[16,128]{1,0:T(8,128)S(1)} %bitcast.70), kind=kOutput, calls=%fused_computation.16 | convolution fusion | flops 469958656 | bytes 18489344 | tf_op jit(solution)/shard_map/sbcd,dbe->sbce/dot_general | solution.py:40
  117.6 10.2 %all_gather.3 = bf16[4,8,64,128]{3,2,1,0:T(8,128)(2,1)S(1)} all-gather(bf16[1,8,64,128]{3,2,1,0:T(8,128)(2,1)S(1)} %copy.42), channel_id=1, replica_groups=mesh['layer'=4,'tok'=8] {'layer'}, dimensions={0}, use_global_device_ids=true | all-gather | bytes 655360 | tf_op jit(solution)/shard_map/all_gather | solution.py:47
  127.8 0.6 gather_fusion.1
  128.5 25.9 %convolution_convert_fusion = bf16[4,16,8,4,3584]{4,2,3,1,0:T(8,128)(2,1)} fusion(bf16[4,16,128,3584,1]{3,2,4,1,0:T(8,128)(2,1)} %bitcast.59, bf16[4,8,16,4,128]{4,3,2,1,0:T(4,128)(2,1)S(1)} %bitcast.64, pred[4]{0:T(512)(128)(4,1)S(1)} %get-tuple-element.3, bf16[4]{0:T(256)(128)(2,1)S(1)} %get-tuple-element.2), kind=kOutput, calls=%fused_computation.7 | convolution fusion | flops 1886912512 | bytes 73924624 | tf_op jit(solution)/shard_map/snbce,sbed->snbcd/dot_general | solution.py:57
  154.4 15.6 %copy.44 = bf16[4,8,64,3584]{3,2,0,1:T(8,128)(2,1)} copy(bf16[4,8,64,3584]{3,1,2,0:T(8,128)(2,1)} %bitcast.58) | data formatting | bytes 29360128 | tf_op jit(solution)/shard_map/reshape | solution.py:64
  170.0 0.0 copy-start.1
  170.0 5.7 all-to-all-start.1
  175.7 0.6 gather_fusion.2
  176.2 0.1 fusion.27
  176.3 0.0 copy-done.1
  176.4 318.0 %all-to-all-done.1 = bf16[4,8,64,3584]{3,2,0,1:T(8,128)(2,1)} async-done(((bf16[4,8,64,3584]{3,2,0,1:T(8,128)(2,1)}), bf16[4,8,64,3584]{3,2,0,1:T(8,128)(2,1)}, u32[]{:S(2)}, u32[]{:S(2)}) %all-to-all-start.1) | async-done | bytes 14680096 | tf_op jit(solution)/shard_map/all_to_all | solution.py:66
  494.4 13.4 %copy.45 = bf16[4,8,64,3584]{3,2,1,0:T(8,128)(2,1)} copy(bf16[4,8,64,3584]{3,2,0,1:T(8,128)(2,1)} %all-to-all-done.1) | data formatting | bytes 29360128 | tf_op jit(solution)/shard_map/all_to_all | solution.py:66
  507.8 32.0 %gather_fusion.3 = bf16[1024,3584]{1,0:T(8,128)(2,1)} fusion(bf16[4,512,3584]{2,1,0:T(8,128)(2,1)} %bitcast.56, s32[1024]{0:T(1024)S(1)} %bitcast.57), kind=kCustom, calls=%fused_computation.3 | custom fusion | bytes 14688256 | tf_op jit(solution)/shard_map/vmap()/gather | solution.py:70
  539.8 16.2 %reshape.172 = f32[4,128,2,3584]{3,2,1,0:T(2,128)} reshape(bf16[1024,3584]{1,0:T(8,128)(2,1)} %gather_fusion.3) | data formatting | bytes 22020096 | tf_op jit(solution)/shard_map/convert_element_type | solution.py:71
  556.0 22.3 %reduce_sum.39 = f32[4,128,3584]{2,1,0:T(8,128)} reduce(f32[4,128,2,3584]{3,2,1,0:T(2,128)} %reshape.172, f32[]{:T(128)} %constant.75.clone.1), dimensions={2}, to_apply=%region_4.5 | reduce | flops 1835008 | bytes 22020100 | tf_op jit(solution)/shard_map/reduce_sum | solution.py:71
  578.3 0.0 copy-start
  578.3 4.3 multiply_reduce_fusion
  582.6 1.0 fusion.4
  583.6 0.0 copy-done
  583.6 0.4 fusion.3
  584.0 0.5 multiply_bitcast_fusion
  (16 shorter events, 0.2 us)
Async XLA Ops:
  11.1 89.2 %all-to-all-start = ((bf16[8,64,3584]{2,1,0:T(8,128)(2,1)}), bf16[8,64,3584]{2,1,0:T(8,128)(2,1)}, u32[]{:S(2)}, u32[]{:S(2)}) async-start(bf16[8,64,3584]{2,1,0:T(8,128)(2,1)} %bitcast.60), calls=%async_computation | async-start | bytes 7340032 | tf_op jit(solution)/shard_map/all_to_all | solution.py:37
  31.9 72.4 %copy-start.2 = (f32[1,2048]{1,0:T(1,128)S(1)}, f32[1,2048]{1,0:T(1,128)}, u32[]{:S(2)}) copy-start(f32[1,2048]{1,0:T(1,128)} %param.11) | copy-start | bytes 24580
  170.0 6.3 %copy-start.1 = (f32[1,3584]{1,0:T(1,128)S(1)}, f32[1,3584]{1,0:T(1,128)}, u32[]{:S(2)}) copy-start(f32[1,3584]{1,0:T(1,128)} %param.13) | copy-start | bytes 43012
  170.0 324.4 %all-to-all-start.1 = ((bf16[4,8,64,3584]{3,2,0,1:T(8,128)(2,1)}), bf16[4,8,64,3584]{3,2,0,1:T(8,128)(2,1)}, u32[]{:S(2)}, u32[]{:S(2)}) async-start(bf16[4,8,64,3584]{3,2,0,1:T(8,128)(2,1)} %copy.44), calls=%async_computation.1 | async-start | bytes 29360128 | tf_op jit(solution)/shard_map/all_to_all | solution.py:66
  578.3 5.3 copy-start
where the time goes:
time: 586 us; the launch traced here: 585 us
  waiting for transfers between devices  386 us (66%)
  local copies, waits for them, and re-layouts  106 us (18%)
  matrix products  39.1 us (7%)
  other arithmetic  30.2 us (5%)
  starting transfers between devices  12 us (2%)
  blocking collectives  10.2 us (2%)
    all_to_all x1, waiting for transfers between devices, body(): lax.all_to_all(terms, 'tok', split_axis=1, concat_axis=1, tiled=True)  318 us
    all_to_all x1, waiting for transfers between devices, body(): lax.all_to_all(outgoing, 'tok', split_axis=0, concat_axis=0, tiled=True)  68.3 us
    gather x1, local copies, waits for them, and re-layouts, body(): rows[where_at]  32 us
    dot_general x1, matrix products, body(): jnp.einsum('snbce,sbed->snbcd', chosen_codes.reshape(slot_sets, tok_count...  25.9 us
    reduce_sum x1, other arithmetic, body(): jnp.sum(picked.astype(jnp.float32).reshape(slot_sets, tok_rows, topk, wid...  22.3 us
    convert_element_type x1, local copies, waits for them, and re-layouts, body(): picked.astype(jnp.float32).reshape(slot_sets, tok_rows, topk, width)  16.2 us
    reshape x1, local copies, waits for them, and re-layouts, body(): terms = jnp.einsum('snbce,sbed->snbcd', chosen_codes.reshape(slot_sets, t...  15.6 us
    unnamed x9, local copies, waits for them, and re-layouts  15.3 us
  transfers between devices with their start and end apart: 2, of which 2 were waited for; matrix products, arithmetic and copies ran while one was open for 3% of the time, Pallas kernels for 0%

commit v1 on v0

--- a/solution.py
+++ b/solution.py
@@ -4,6 +4,26 @@
 from jax.sharding import PartitionSpec as P
 
 BLOCK = 128
+
+
+def _push_counts(m, axis_key, out_dim, where_dim):
+    shaped, z_new = (lax.psum(1, axis_key), lax.axis_index(axis_key))
+    later = m.shape[out_dim] // shaped
+    state_now = list(m.shape)
+    state_now[out_dim] = later
+    last = state_now[where_dim]
+    state_now[where_dim] = last * shaped
+    block_last = jnp.zeros(state_now, m.dtype)
+    for rr in range(shaped):
+        back = lax.dynamic_slice_in_dim(m, (z_new ^ rr) * later, later, axis=out_dim)
+        if rr:
+            back = lax.ppermute(
+                back, axis_key, list(map(lambda tick: (tick, tick ^ rr), range(shaped)))
+            )
+        block_last = lax.dynamic_update_slice_in_dim(
+            block_last, back, (z_new ^ rr) * last, axis=where_dim
+        )
+    return block_last
 
 
 def slot_positions(ids, blocks, capacity):
@@ -63,9 +83,7 @@
         .astype(jnp.bfloat16)
         .reshape(slot_sets, tok_count, per_owner * capacity, width)
     )
-    returned = lax.all_to_all(terms, "tok", split_axis=1, concat_axis=1, tiled=True).reshape(
-        slot_sets, slot_count, width
-    )
+    returned = _push_counts(terms, "tok", 1, 1).reshape(slot_sets, slot_count, width)
     source_positions = jnp.take(positions, sources, axis=0)
     picked = jax.vmap(lambda rows, where_at: rows[where_at])(returned, source_positions)
     parts = jnp.sum(picked.astype(jnp.float32).reshape(slot_sets, tok_rows, topk, width), axis=2)

time: 586 us -> 612 us (1.044)
  the two profiles are of different devices: /device:TPU:0 before, /device:TPU:11 now
where the time goes in v1:
time: 612 us; the launch traced here: 611 us
  waiting for transfers between devices  349 us (57%)
  local copies, waits for them, and re-layouts  166 us (27%)
  matrix products  39.2 us (6%)
  other arithmetic  30.2 us (5%)
  starting transfers between devices  17.2 us (3%)
  blocking collectives  8.25 us (1%)
    ppermute x7, waiting for transfers between devices, _push_counts(): lax.ppermute(back, axis_key, list(map(lambda tick: (tick, tick ^ rr), ran...  284 us
    all_to_all x1, waiting for transfers between devices, body(): lax.all_to_all(outgoing, 'tok', split_axis=0, concat_axis=0, tiled=True)  64.7 us
    dynamic_slice x1, local copies, waits for them, and re-layouts, _push_counts(): lax.dynamic_slice_in_dim(m, (z_new ^ rr) * later, later, axis=out_dim)  50.2 us
    gather x1, local copies, waits for them, and re-layouts, body(): rows[where_at]  31.9 us
    unnamed x26, local copies, waits for them, and re-layouts  29.3 us
    dot_general x1, matrix products, body(): jnp.einsum('snbce,sbed->snbcd', chosen_codes.reshape(slot_sets, tok_count...  25.9 us
    reduce_sum x1, other arithmetic, body(): jnp.sum(picked.astype(jnp.float32).reshape(slot_sets, tok_rows, topk, wid...  22.3 us
    dynamic_update_slice x8, local copies, waits for them, and re-layouts, _push_counts(): lax.dynamic_update_slice_in_dim(block_last, back, (z_new ^ rr) * last, ax...  19.4 us
  transfers between devices with their start and end apart: 8, of which 6 were waited for; matrix products, arithmetic and copies ran while one was open for 8% of the time, Pallas kernels for 0%

profile of v1, /device:TPU:11, one launch (start us, length us, event | category | flops | bytes accessed | tf_op | source)
XLA Modules:
  0.0 610.7 jit_solution(2666494704854561816)
XLA Ops:
  0.7 0.9 copy.54
  1.6 1.0 copy.58
  2.6 0.9 fusion.14
  3.8 0.4 fusion.16
  4.3 1.4 scatter_custom_fusion
  5.8 4.2 gather_fusion
  10.0 5.6 all-to-all-start
  15.6 14.5 %copy.83 = bf16[448,8,16,128]{3,2,1,0:T(8,128)(2,1)} copy(bf16[448,8,16,128]{3,1,2,0:T(8,128)(2,1)} %bitcast.63) | data formatting | bytes 29360128
  30.2 64.7 %all-to-all-done = bf16[8,64,3584]{2,1,0:T(8,128)(2,1)} async-done(((bf16[8,64,3584]{2,1,0:T(8,128)(2,1)}), bf16[8,64,3584]{2,1,0:T(8,128)(2,1)}, u32[]{:S(2)}, u32[]{:S(2)}) %all-to-all-start) | async-done | bytes 3670048 | tf_op jit(solution)/shard_map/all_to_all | solution.py:57
  94.9 4.1 copy.60
  98.9 13.2 %fusion.11 = bf16[16,8,4,128]{3,1,2,0:T(8,128)(2,1)S(1)} fusion(bf16[8,16,4,3584]{3,0,2,1:T(8,128)(2,1)S(1)} %bitcast.65, bf16[3584,16,128,1]{2,1,0,3:T(8,128)(2,1)} %bitcast.64, f32[16,128]{1,0:T(8,128)S(1)} %bitcast.72), kind=kOutput, calls=%fused_computation.17 | convolution fusion | flops 469958656 | bytes 18489344 | tf_op jit(solution)/shard_map/sbcd,dbe->sbce/dot_general | solution.py:60
  112.2 8.3 %all_gather.3 = bf16[4,8,64,128]{3,2,1,0:T(8,128)(2,1)S(1)} all-gather(bf16[1,8,64,128]{3,2,1,0:T(8,128)(2,1)S(1)} %copy.62), channel_id=1, replica_groups=mesh['layer'=4,'tok'=8] {'layer'}, dimensions={0}, use_global_device_ids=true | all-gather | bytes 655360 | tf_op jit(solution)/shard_map/all_gather | solution.py:67
  120.4 0.6 gather_fusion.1
  121.1 25.9 %convolution_convert_fusion = bf16[4,16,8,4,3584]{4,2,3,1,0:T(8,128)(2,1)} fusion(bf16[4,16,128,3584,1]{3,2,4,1,0:T(8,128)(2,1)} %bitcast.61, bf16[4,8,16,4,128]{4,3,2,1,0:T(4,128)(2,1)S(1)} %bitcast.66, pred[4]{0:T(512)(128)(4,1)S(1)} %get-tuple-element.11, bf16[4]{0:T(256)(128)(2,1)S(1)} %get-tuple-element.10), kind=kOutput, calls=%fused_computation.7 | convolution fusion | flops 1886912512 | bytes 73924624 | tf_op jit(solution)/shard_map/snbce,sbed->snbcd/dot_general | solution.py:77
  147.0 50.2 %constant_dynamic-slice_fusion = (bf16[4,1,64,3584]{3,1,2,0:T(2,128)(2,1)}, bf16[4,1,64,3584]{3,1,2,0:T(2,128)(2,1)}, bf16[4,1,64,3584]{3,1,2,0:T(2,128)(2,1)}, ...) fusion(bf16[4,8,64,3584]{3,1,2,0:T(8,128)(2,1)} %bitcast.59, ...), kind=kLoop, calls=%fused_computation.36 | loop fusion | bytes 29360160 | tf_op jit(solution)/shard_map/dynamic_slice | solution.py:18
  197.2 1.5 copy.76
  198.6 2.5 collective-permute-start
  201.1 0.6 gather_fusion.2
  201.7 3.5 copy.77
  205.2 3.5 collective-permute-start.1
  208.8 3.7 copy.78
  212.5 1.5 copy.79
  214.0 1.2 collective-permute-start.3
  215.3 1.5 copy.80
  216.7 1.7 collective-permute-start.4
  218.4 6.9 %broadcast_in_dim.37 = bf16[4,8,64,3584]{3,2,1,0:T(8,128)(2,1)} broadcast(bf16[]{:T(256)} %constant.38.clone.1), dimensions={} | broadcast | bytes 14680066 | tf_op jit(solution)/shard_map/broadcast_in_dim | solution.py:16
  225.3 3.7 copy_dynamic-update-slice_fusion
  229.2 1.8 copy-done
  231.4 2.9 constant_dynamic-update-slice_fusion.6
  234.3 84.3 %collective-permute-done.1 = bf16[4,1,64,3584]{3,2,1,0:T(8,128)(2,1)S(1)} collective-permute-done((bf16[4,1,64,3584]{3,2,1,0:T(8,128)(2,1)}, bf16[4,1,64,3584]{3,2,1,0:T(8,128)(2,1)S(1)}, u32[]{:S(2)}, u32[]{:S(2)}) %collective-permute-start.1) | collective-permute-done | bytes 1835040 | tf_op jit(solution)/shard_map/ppermute | solution.py:20
  318.6 2.6 collective-permute-start.6
  321.2 1.3 constant_dynamic-update-slice_fusion.5
  322.5 35.4 %collective-permute-done.2 = bf16[4,1,64,3584]{3,2,1,0:T(8,128)(2,1)} collective-permute-done((bf16[4,1,64,3584]{3,2,1,0:T(8,128)(2,1)}, bf16[4,1,64,3584]{3,2,1,0:T(8,128)(2,1)}, u32[]{:S(2)}, u32[]{:S(2)}) %collective-permute-start.2) | collective-permute-done | bytes 1835040 | tf_op jit(solution)/shard_map/ppermute | solution.py:20
  357.9 2.9 constant_dynamic-update-slice_fusion.4
  360.8 2.9 constant_dynamic-update-slice_fusion.3
  363.7 87.7 %collective-permute-done.4 = bf16[4,1,64,3584]{3,2,1,0:T(8,128)(2,1)} collective-permute-done((bf16[4,1,64,3584]{3,2,1,0:T(8,128)(2,1)}, bf16[4,1,64,3584]{3,2,1,0:T(8,128)(2,1)}, u32[]{:S(2)}, u32[]{:S(2)}) %collective-permute-start.4) | collective-permute-done | bytes 1835040 | tf_op jit(solution)/shard_map/ppermute | solution.py:20
  451.4 2.8 constant_dynamic-update-slice_fusion.2
  454.3 38.7 %collective-permute-done.5 = bf16[4,1,64,3584]{3,2,1,0:T(8,128)(2,1)S(1)} collective-permute-done((bf16[4,1,64,3584]{3,2,1,0:T(8,128)(2,1)S(1)}, bf16[4,1,64,3584]{3,2,1,0:T(8,128)(2,1)S(1)}, u32[]{:S(2)}, u32[]{:S(2)}) %collective-permute-start.5) | collective-permute-done | bytes 1835040 | tf_op jit(solution)/shard_map/ppermute | solution.py:20
  493.0 1.4 constant_dynamic-update-slice_fusion.1
  494.4 38.3 %collective-permute-done.6 = bf16[4,1,64,3584]{3,2,1,0:T(8,128)(2,1)S(1)} collective-permute-done((bf16[4,1,64,3584]{3,2,1,0:T(8,128)(2,1)S(1)}, bf16[4,1,64,3584]{3,2,1,0:T(8,128)(2,1)S(1)}, u32[]{:S(2)}, u32[]{:S(2)}) %collective-permute-start.6) | collective-permute-done | bytes 1835040 | tf_op jit(solution)/shard_map/ppermute | solution.py:20
  532.6 1.4 constant_dynamic-update-slice_fusion
  534.1 31.9 %gather_fusion.3 = bf16[1024,3584]{1,0:T(8,128)(2,1)} fusion(bf16[4,512,3584]{2,1,0:T(8,128)(2,1)} %bitcast.58, s32[1024]{0:T(1024)S(1)} %bitcast.60), kind=kCustom, calls=%fused_computation.3 | custom fusion | bytes 14688256 | tf_op jit(solution)/shard_map/vmap()/gather | solution.py:88
  566.0 16.2 %reshape.172 = f32[4,128,2,3584]{3,2,1,0:T(2,128)} reshape(bf16[1024,3584]{1,0:T(8,128)(2,1)} %gather_fusion.3) | data formatting | bytes 22020096 | tf_op jit(solution)/shard_map/convert_element_type | solution.py:89
  582.1 22.3 %reduce_sum.39 = f32[4,128,3584]{2,1,0:T(8,128)} reduce(f32[4,128,2,3584]{3,2,1,0:T(2,128)} %reshape.172, f32[]{:T(128)} %constant.85.clone.1), dimensions={2}, to_apply=%region_4.5 | reduce | flops 1835008 | bytes 22020100 | tf_op jit(solution)/shard_map/reduce_sum | solution.py:89
  604.5 4.3 multiply_reduce_fusion
  608.7 1.0 fusion.4
  609.8 0.4 fusion.3
  610.2 0.5 multiply_bitcast_fusion
  (41 shorter events, 1.2 us)
Async XLA Ops:
  0.6 5.1 copy-start.4
  10.0 84.9 %all-to-all-start = ((bf16[8,64,3584]{2,1,0:T(8,128)(2,1)}), bf16[8,64,3584]{2,1,0:T(8,128)(2,1)}, u32[]{:S(2)}, u32[]{:S(2)}) async-start(bf16[8,64,3584]{2,1,0:T(8,128)(2,1)} %bitcast.62), calls=%async_computation | async-start | bytes 7340032 | tf_op jit(solution)/shard_map/all_to_all | solution.py:57
  30.2 68.8 %copy-start.7 = (f32[1,2048]{1,0:T(1,128)S(1)}, f32[1,2048]{1,0:T(1,128)}, u32[]{:S(2)}) copy-start(f32[1,2048]{1,0:T(1,128)} %param.11) | copy-start | bytes 24580
  198.6 10.1 %copy-start.6 = (f32[1,3584]{1,0:T(1,128)S(1)}, f32[1,3584]{1,0:T(1,128)}, u32[]{:S(2)}) copy-start(f32[1,3584]{1,0:T(1,128)} %param.13) | copy-start | bytes 43012
  198.6 32.6 %collective-permute-start = (bf16[4,1,64,3584]{3,2,1,0:T(8,128)(2,1)}, bf16[4,1,64,3584]{3,2,1,0:T(8,128)(2,1)}, u32[]{:S(2)}, u32[]{:S(2)}) collective-permute-start(bf16[4,1,64,3584]{3,2,1,0:T(8,128)(2,1)} %copy.76), channel_id=1, source_target_pairs={{0,1},{1,0},{2,3},{3,2},{4,5},{5,4},{6,7},{7,6},{8,9},{9,8},{10,11... | collective-permute-start | bytes 5505032 | tf_op jit(solution)/shard_map/ppermute | solution.py:20
  205.2 113.4 %collective-permute-start.1 = (bf16[4,1,64,3584]{3,2,1,0:T(8,128)(2,1)}, bf16[4,1,64,3584]{3,2,1,0:T(8,128)(2,1)S(1)}, u32[]{:S(2)}, u32[]{:S(2)}) collective-permute-start(bf16[4,1,64,3584]{3,2,1,0:T(8,128)(2,1)} %copy.77), channel_id=1, source_target_pairs={{0,2},{1,3},{2,0},{3,1},{4,6},{5,7},{6,4},{7,5},{8,10},{9,11},{10,... | collective-permute-start | bytes 5505032 | tf_op jit(solution)/shard_map/ppermute | solution.py:20
  208.8 3.7 copy-start.3
  212.5 2.7 copy-start.2
  212.5 145.4 %collective-permute-start.2 = (bf16[4,1,64,3584]{3,2,1,0:T(8,128)(2,1)}, bf16[4,1,64,3584]{3,2,1,0:T(8,128)(2,1)}, u32[]{:S(2)}, u32[]{:S(2)}) collective-permute-start(bf16[4,1,64,3584]{3,2,1,0:T(8,128)(2,1)} %copy.78), channel_id=1, source_target_pairs={{0,3},{1,2},{2,1},{3,0},{4,7},{5,6},{6,5},{7,4},{8,11},{9,10},{10,... | collective-permute-start | bytes 5505032 | tf_op jit(solution)/shard_map/ppermute | solution.py:20
  214.0 146.8 %collective-permute-start.3 = (bf16[4,1,64,3584]{3,2,1,0:T(8,128)(2,1)}, bf16[4,1,64,3584]{3,2,1,0:T(8,128)(2,1)}, u32[]{:S(2)}, u32[]{:S(2)}) collective-permute-start(bf16[4,1,64,3584]{3,2,1,0:T(8,128)(2,1)} %copy.79), channel_id=1, source_target_pairs={{0,4},{1,5},{2,6},{3,7},{4,0},{5,1},{6,2},{7,3},{8,12},{9,13},{10,... | collective-permute-start | bytes 5505032 | tf_op jit(solution)/shard_map/ppermute | solution.py:20
  216.7 234.7 %collective-permute-start.4 = (bf16[4,1,64,3584]{3,2,1,0:T(8,128)(2,1)}, bf16[4,1,64,3584]{3,2,1,0:T(8,128)(2,1)}, u32[]{:S(2)}, u32[]{:S(2)}) collective-permute-start(bf16[4,1,64,3584]{3,2,1,0:T(8,128)(2,1)} %copy.80), channel_id=1, source_target_pairs={{0,5},{1,4},{2,7},{3,6},{4,1},{5,0},{6,3},{7,2},{8,13},{9,12},{10,... | collective-permute-start | bytes 5505032 | tf_op jit(solution)/shard_map/ppermute | solution.py:20
  225.3 3.7 copy-start.1
  229.0 2.0 copy-start
  231.3 261.7 %collective-permute-start.5 = (bf16[4,1,64,3584]{3,2,1,0:T(8,128)(2,1)S(1)}, bf16[4,1,64,3584]{3,2,1,0:T(8,128)(2,1)S(1)}, u32[]{:S(2)}, u32[]{:S(2)}) collective-permute-start(bf16[4,1,64,3584]{3,2,1,0:T(8,128)(2,1)S(1)} %copy.81), channel_id=1, source_target_pairs={{0,6},{1,7},{2,4},{3,5},{4,2},{5,3},{6,0},{7,1},{8,14},{9,15},{10,... | collective-permute-start | bytes 5505032 | tf_op jit(solution)/shard_map/ppermute | solution.py:20
  318.6 214.1 %collective-permute-start.6 = (bf16[4,1,64,3584]{3,2,1,0:T(8,128)(2,1)S(1)}, bf16[4,1,64,3584]{3,2,1,0:T(8,128)(2,1)S(1)}, u32[]{:S(2)}, u32[]{:S(2)}) collective-permute-start(bf16[4,1,64,3584]{3,2,1,0:T(8,128)(2,1)S(1)} %copy.82), channel_id=1, source_target_pairs={{0,7},{1,6},{2,5},{3,4},{4,3},{5,2},{6,1},{7,0},{8,15},{9,14},{10,... | collective-permute-start | bytes 5505032 | tf_op jit(solution)/shard_map/ppermute | solution.py:20
  604.5 5.3 copy-start.5
